TPU v7x, 256 devices: a whole 4x4x8 slice. The times are simulated.
256 devices in a mesh: own: 32 (over x, z), row: 8 (over y, core).
Axes of the slice: x: 4, y: 4, z: 8, core: 2. Of those that a mesh axis runs over, the one named last changes fastest.
Arguments:
- sigma_anc: float32 [16384, 16384], P('row', 'own'), may hold values from -1.5 to 1.5
- row_blocks: int32 [64, 8], replicated, may hold values from 0 to 63, as said below
- panel1: float32 [64, 2048, 256], P('own', 'row'), may hold values from -0.375 to 0.375
- diag_inv1: float32 [64, 256, 256], P('own'), as said below
- mask1: int32 [64, 8], P('own', 'row'), may hold values 0 or 1
- parent_block2: float32 [64, 256, 256], P('own'), may hold values from -0.375 to 0.375
- panel2: float32 [64, 2048, 256], P('own', 'row'), may hold values from -0.375 to 0.375
- diag_inv2: float32 [64, 256, 256], P('own'), as said below
- mask2: int32 [64, 8], P('own', 'row'), may hold values 0 or 1
Outputs:
- sel1_panel: float32 [64, 2048, 256], P('own', 'row')
- sel1_diag: float32 [64, 256, 256], P('own')
- sel2_parent: float32 [64, 256, 256], P('own')
- sel2_panel: float32 [64, 2048, 256], P('own', 'row')
- sel2_diag: float32 [64, 256, 256], P('own')
Inputs may be any that keep to these rules, and one draw needn't show every extreme that they name: `row_blocks`: entry l of each row lies in block rows 8 * l to 8 * (l + 1) - 1; for supernodes s with the same s // 2, the entries of one column l lie in different aligned runs of 2 block rows. `diag_inv1`: lower triangular, with diagonal entries from 1 to 2. `diag_inv2`: lower triangular, with diagonal entries from 1 to 2.
All inputs are finite; a program needn't handle non-finite values. No bound on the sum of `mask1` or of `mask2` on one device may be relied on, other than what follows from the above.
Results may differ from a plain program's by a relative error of at most 0.000071.
Values sent between devices are 32-bit elements; how exact they have to be, the bound alone decides.
No kernel may reach another device: no remote copies, remote signals or barrier semaphores. Data moves between devices by JAX's collectives and lax.ppermute only.
A program may use at most 128 MiB of HBM per device.

v0:
```python
import jax
import jax.numpy as jnp
from jax import lax
from jax.sharding import PartitionSpec as P

B = 256
HIGH = lax.Precision.HIGHEST


def shifted(shard, axis, by):
    length = lax.axis_size(axis)
    return lax.ppermute(shard, axis, [(i, (i + by) % length) for i in range(length)])


def product(form, left, right):
    return jnp.einsum(form, left, right, precision=HIGH)


def select_send(sigma_local, row_blocks, slots):
    own_count = lax.axis_size("own")
    own_here = lax.axis_index("own")
    row_here = lax.axis_index("row")
    rows_here = sigma_local.shape[0] // B
    cols_here = sigma_local.shape[1] // B
    rowlist = row_blocks.reshape(own_count, slots, -1)
    group = own_here * cols_here // rows_here
    want_col = lax.dynamic_index_in_dim(rowlist, group, 2, keepdims=False)
    local_col = want_col - own_here * cols_here
    match = ((local_col >= 0) & (local_col < cols_here)).astype(jnp.int32)
    which = jnp.sum(match * jnp.arange(slots, dtype=jnp.int32)[None, :], axis=1)
    chosen = rowlist[jnp.arange(own_count, dtype=jnp.int32), which]
    chosen_row = (
        lax.dynamic_index_in_dim(chosen, row_here, 1, keepdims=False) - row_here * rows_here
    )
    chosen_col = jnp.clip(
        lax.dynamic_index_in_dim(chosen, group, 1, keepdims=False) - own_here * cols_here,
        0,
        cols_here - 1,
    )
    blocks4 = sigma_local.reshape(rows_here, B, cols_here, B)
    return blocks4[chosen_row, :, chosen_col, :]


def select_take(received, row_blocks, slots, cols_here):
    mine = lax.axis_index("own") * slots + jnp.arange(slots, dtype=jnp.int32)
    rowlist = row_blocks[mine]
    sender = rowlist // cols_here
    return received[sender]


def on_device(
    sigma_anc, row_blocks, panel1, diag_inv1, mask1, parent_block2, panel2, diag_inv2, mask2
):
    slots = panel1.shape[0]
    cols_here = sigma_anc.shape[1] // B
    keep_own2 = mask2.astype(jnp.float32)
    up_parent = product("kij,kjc->kic", parent_block2, diag_inv2)
    factor2_own = keep_own2[:, :, None] * product("kij,kjc->kic", panel2, diag_inv2)
    factor2_child = shifted(factor2_own, "own", -1)
    outgoing = select_send(sigma_anc, row_blocks, slots)
    received = lax.all_to_all(outgoing, "own", split_axis=0, concat_axis=0, tiled=True)
    blocks1 = select_take(received, row_blocks, slots, cols_here)
    keep1 = mask1.astype(jnp.float32)
    factor1 = keep1[:, :, None] * product("kij,kjc->kic", panel1, diag_inv1)
    factors1 = lax.all_gather(factor1, "row", axis=1, tiled=True).reshape(slots, -1, B, B)
    sel1_panel = -keep1[:, :, None] * product("kmij,kmjc->kic", blocks1, factors1)
    gram1 = product("kji,kjc->kic", diag_inv1, diag_inv1)
    sel1_diag = gram1 - lax.psum(product("kji,kjc->kic", factor1, sel1_panel), "row")
    factor2 = keep1[:, :, None] * factor2_child
    factors2 = lax.all_gather(factor2, "row", axis=1, tiled=True).reshape(slots, -1, B, B)
    anc2 = keep1[:, :, None] * product("kmij,kmjc->kic", blocks1, factors2)
    par_panel = shifted(sel1_panel, "own", 1)
    par_anc = shifted(anc2, "own", 1)
    par_diag = shifted(sel1_diag, "own", 1)
    sel2_panel = -keep_own2[:, :, None] * (product("kij,kjc->kic", par_panel, up_parent) + par_anc)
    cross = product("kji,kjc->kic", par_panel, factor2_own)
    back = product("kji,kjc->kic", factor2_own, sel2_panel)
    par_diag, cross, back = lax.optimization_barrier((par_diag, cross, back))
    cross, back = lax.psum((cross, back), "row")
    sel2_parent = -(product("kij,kjc->kic", par_diag, up_parent) + cross)
    gram2 = product("kji,kjc->kic", diag_inv2, diag_inv2)
    sel2_diag = gram2 - product("kji,kjc->kic", up_parent, sel2_parent) - back
    return (sel1_panel, sel1_diag, sel2_parent, sel2_panel, sel2_diag)


def solution(mesh):
    in_specs = (
        P("row", "own"),
        P(),
        P("own", "row", None),
        P("own", None, None),
        P("own", "row"),
        P("own", None, None),
        P("own", "row", None),
        P("own", None, None),
        P("own", "row"),
    )
    out_specs = (
        P("own", "row", None),
        P("own", None, None),
        P("own", None, None),
        P("own", "row", None),
        P("own", None, None),
    )
    return jax.shard_map(
        on_device, mesh=mesh, in_specs=in_specs, out_specs=out_specs, check_vma=False
    )
```

profile of v0, /device:TPU:2, one launch (start us, length us, event | category | flops | bytes accessed | tf_op | source)
XLA Modules:
  0.0 444.9 jit_solution(6164868798614665549)
XLA Ops:
  7.2 0.0 copy-start
  7.2 0.8 copy.67
  8.0 0.1 constant_dynamic-slice_fusion
  8.1 0.1 copy.90
  8.2 0.1 copy.69
  8.3 0.1 fusion.7
  8.5 0.7 gather_fusion
  9.1 5.9 %reshape.167 = f32[8,256,2,256]{3,2,1,0:T(2,128)} reshape(f32[2048,512]{1,0:T(8,128)} %param.9) | data formatting | bytes 8388608 | tf_op jit(solution)/shard_map/reshape | solution.py:40
  15.1 4.7 %copy.72 = f32[8,256,2,256]{3,1,2,0:T(8,128)} copy(f32[8,256,2,256]{3,2,1,0:T(2,128)} %reshape.167) | data formatting | bytes 8388608 | tf_op jit(solution)/shard_map/reshape | solution.py:40
  19.7 0.2 fusion.11
  19.9 6.5 %gather_fusion.1 = f32[32,256,256]{2,1,0:T(8,128)} fusion(f32[8,256,2,256]{3,1,2,0:T(8,128)} %copy.72, s32[32]{0:T(128)S(1)} %fusion.11), kind=kCustom, calls=%fused_computation.1 | custom fusion | bytes 16777472 | tf_op jit(solution)/shard_map/gather | solution.py:41
  26.4 0.0 copy-start.8
  26.5 11.8 %all-to-all-start = ((f32[32,256,256]{2,1,0:T(8,128)}), f32[32,256,256]{2,1,0:T(8,128)}, u32[]{:S(2)}, u32[]{:S(2)}) async-start(f32[32,256,256]{2,1,0:T(8,128)} %gather_fusion.1), calls=%async_computation | async-start | bytes 16777216 | tf_op jit(solution)/shard_map/all_to_all | solution.py:61
  38.3 0.0 all-gather.3.cloned.1.call-start
  38.3 0.0 copy-done.9
  38.3 0.0 copy-done.2
  38.4 0.0 copy-done.7
  38.4 1.5 convolution_multiply_fusion.1
  39.8 0.0 all-gather.3.cloned.1.call-update
  39.8 0.0 all-gather.5.cloned.1.call-start
  39.9 0.0 copy-done.10
  39.9 0.0 copy-done
  39.9 0.0 copy-done.8
  39.9 0.7 convolution_multiply_fusion
  40.6 2.8 collective-permute-start.2
  43.3 190.9 %collective-permute-done.2 = f32[2,256,256]{2,1,0:T(8,128)S(1)} collective-permute-done((f32[2,256,256]{2,1,0:T(8,128)S(1)}, f32[2,256,256]{2,1,0:T(8,128)S(1)}, u32[]{:S(2)}, u32[]{:S(2)}) %collective-permute-start.2) | collective-permute-done | bytes 524320 | tf_op jit(solution)/shard_map/ppermute | solution.py:12
  234.2 0.9 broadcast_multiply_fusion
  235.1 0.0 all-gather.5.cloned.1.call-update
  235.1 0.0 all-reduce.4.cloned.1.call-start
  235.2 0.6 gather_fusion.2
  235.8 0.1 reshape.158
  235.9 0.0 all-to-all-done
  235.9 6.2 %gather_fusion.3 = f32[16,256,256]{2,1,0:T(8,128)} fusion(f32[32,256,256]{2,1,0:T(8,128)} %all-to-all-done, s32[1024]{0:T(1024)S(1)} %pad_clamp_fusion), kind=kCustom, calls=%fused_computation.3 | custom fusion | bytes 8388672 | tf_op jit(solution)/shard_map/gather | solution.py:48
  242.1 8.1 %fusion.3 = f32[2,256,256]{2,1,0:T(8,128)S(1)} fusion(f32[2,8,256,256]{3,2,1,0:T(8,128)} %bitcast.67, f32[2,8,256,256]{3,2,1,0:T(8,128)} %bitcast.69, f32[2]{0:T(128)S(1)} %fusion.16), kind=kOutput, calls=%fused_computation.14 | convolution fusion | flops 3221356544 | bytes 8912904 | tf_op jit(solution)/shard_map/kmij,kmjc->kic/dot_general | solution.py:16
  250.2 0.0 copy-start.3
  250.2 0.3 collective-permute-start.1
  250.5 0.0 copy-done.1
  250.5 1.9 fusion.18
  252.4 21.4 %all-gather.5.cloned.1.call-done = f32[2,2048,256]{2,1,0:T(8,128)} async-done(((f32[2,256,256]{2,1,0:T(8,128)}), f32[2,2048,256]{2,1,0:T(8,128)}) %all-gather.5.cloned.1.call-update) | async-done | bytes 4194320 | tf_op jit(solution)/shard_map/all_gather | solution.py:70
  273.8 8.2 %fusion.1 = f32[2,256,256]{2,1,0:T(8,128)} fusion(f32[2,8,256,256]{3,2,1,0:T(8,128)} %bitcast.68, f32[2,8,256,256]{3,2,1,0:T(8,128)} %bitcast.70, f32[2]{0:T(128)S(1)} %convert_bitcast_fusion.1), kind=kOutput, calls=%fused_computation.8 | convolution fusion | flops 3221356544 | bytes 8912904 | tf_op jit(solution)/shard_map/kmij,kmjc->kic/dot_general | solution.py:16
  282.0 0.0 copy-done.3
  282.0 1.5 collective-permute-start.3
  283.6 0.0 all-reduce.4.cloned.1.call-update
  283.6 0.0 all-reduce.6.cloned.1.call-start
  283.7 1.7 fusion.20
  285.4 63.5 %all-reduce.4.cloned.1.call-done = f32[2,256,256]{2,1,0:T(8,128)} async-done(((f32[2,256,256]{2,1,0:T(8,128)}), f32[2,256,256]{2,1,0:T(8,128)}) %all-reduce.4.cloned.1.call-update) | async-done | bytes 524304 | tf_op jit(solution)/shard_map/psum | solution.py:68
  348.9 2.9 convolution_subtract_fusion.1
  351.8 1.6 collective-permute-start
  353.3 0.0 collective-permute-done.3
  353.3 0.0 collective-permute-done.1
  353.3 1.7 fusion.2
  355.0 0.0 copy-start.4
  355.0 1.8 fusion.21
  356.9 1.8 fusion.19
  358.7 7.1 %collective-permute-done = f32[2,256,256]{2,1,0:T(8,128)} collective-permute-done((f32[2,256,256]{2,1,0:T(8,128)}, f32[2,256,256]{2,1,0:T(8,128)}, u32[]{:S(2)}, u32[]{:S(2)}) %collective-permute-start) | collective-permute-done | bytes 524320 | tf_op jit(solution)/shard_map/ppermute | solution.py:12
  365.8 0.0 all-reduce.6.cloned.1.call-update
  365.8 1.1 fusion.22
  366.9 67.6 %all-reduce.6.cloned.1.call-done = (f32[2,256,256]{2,1,0:T(8,128)}, f32[2,256,256]{2,1,0:T(8,128)}) async-done(((f32[2,256,256]{2,1,0:T(8,128)}, f32[2,256,256]{2,1,0:T(8,128)}), (f32[2,256,256]{2,1,0:T(8,128)}, f32[2,256,256]{2,1,0:T(8,128)})) %all-reduce.6.cloned.1.call-update) | async-done | bytes 1048592 | tf_op jit(solution)/shard_map/psum | solution.py:79
  434.5 1.9 fusion
  436.4 0.0 copy-start.5
  436.4 1.0 convolution_subtract_fusion
  437.5 0.0 copy-done.4
  437.5 0.0 copy-done.6
  437.5 0.9 sub.48
  (17 shorter events, 0.1 us)
Async XLA Ops:
  7.2 32.7 %copy-start = (f32[2,256,256]{2,1,0:T(8,128)S(1)}, f32[2,256,256]{2,1,0:T(8,128)}, u32[]{:S(2)}) copy-start(f32[2,256,256]{2,1,0:T(8,128)} %param.16) | copy-start | bytes 1572868
  26.4 11.9 %copy-start.9 = (s32[2,1]{0,1:T(1,128)S(1)}, s32[2,1]{0,1:T(1,128)}, u32[]{:S(2)}) copy-start(s32[2,1]{0,1:T(1,128)} %param.13) | copy-start | bytes 28
  26.4 11.9 %copy-start.2 = (f32[2,256,256]{2,1,0:T(8,128)S(1)}, f32[2,256,256]{2,1,0:T(8,128)}, u32[]{:S(2)}) copy-start(f32[2,256,256]{2,1,0:T(8,128)} %param.12) | copy-start | bytes 1572868
  26.4 11.9 %copy-start.7 = (f32[2,256,256]{2,1,0:T(8,128)S(1)}, f32[2,256,256]{2,1,0:T(8,128)}, u32[]{:S(2)}) copy-start(f32[2,256,256]{2,1,0:T(8,128)} %param.11) | copy-start | bytes 1572868
  26.4 13.5 %copy-start.10 = (s32[2,1]{0,1:T(1,128)S(1)}, s32[2,1]{0,1:T(1,128)}, u32[]{:S(2)}) copy-start(s32[2,1]{0,1:T(1,128)} %param.17) | copy-start | bytes 28
  26.4 13.5 %copy-start.8 = (f32[2,256,256]{2,1,0:T(8,128)S(1)}, f32[2,256,256]{2,1,0:T(8,128)}, u32[]{:S(2)}) copy-start(f32[2,256,256]{2,1,0:T(8,128)} %param.15) | copy-start | bytes 1572868
  26.5 209.4 %all-to-all-start = ((f32[32,256,256]{2,1,0:T(8,128)}), f32[32,256,256]{2,1,0:T(8,128)}, u32[]{:S(2)}, u32[]{:S(2)}) async-start(f32[32,256,256]{2,1,0:T(8,128)} %gather_fusion.1), calls=%async_computation | async-start | bytes 16777216 | tf_op jit(solution)/shard_map/all_to_all | solution.py:61
  38.3 203.8 %all-gather.3.cloned.1.call-start = ((), (), s32[]{:S(2)}) async-start(), calls=%async_computation.1 | async-start | bytes 4718592 | tf_op jit(solution)/shard_map/all_gather | solution.py:65
  39.8 234.0 %all-gather.5.cloned.1.call-start = ((), (), s32[]{:S(2)}) async-start(), calls=%async_computation.3 | async-start | bytes 4718592 | tf_op jit(solution)/shard_map/all_gather | solution.py:70
  40.6 193.6 %collective-permute-start.2 = (f32[2,256,256]{2,1,0:T(8,128)S(1)}, f32[2,256,256]{2,1,0:T(8,128)S(1)}, u32[]{:S(2)}, u32[]{:S(2)}) collective-permute-start(f32[2,256,256]{2,1,0:T(8,128)S(1)} %convolution_multiply_fusion), channel_id=1, source_target_pairs={{0,248},{8,0},{16,8},{24,16},{32,24},{40,32},{48,40},{56,48},{64,5... | collective-permute-start | bytes 1572872 | tf_op jit(solution)/shard_map/ppermute | solution.py:12
  235.1 113.7 %all-reduce.4.cloned.1.call-start = ((), (), s32[]{:S(2)}) async-start(), calls=%async_computation.2 | async-start | bytes 1048576 | tf_op jit(solution)/shard_map/psum | solution.py:68
  242.1 8.4 %copy-start.1 = (f32[2,256,256]{2,1,0:T(8,128)S(1)}, f32[2,256,256]{2,1,0:T(8,128)}, u32[]{:S(2)}) copy-start(f32[2,256,256]{2,1,0:T(8,128)} %convolution_multiply_fusion.1) | copy-start | bytes 1572868
  250.2 31.8 %copy-start.3 = (f32[2,256,256]{2,1,0:T(8,128)}, f32[2,256,256]{2,1,0:T(8,128)S(1)}, u32[]{:S(2)}) copy-start(f32[2,256,256]{2,1,0:T(8,128)S(1)} %fusion.3) | copy-start | bytes 1572868
  250.2 103.1 %collective-permute-start.1 = (f32[2,256,256]{2,1,0:T(8,128)S(1)}, f32[2,256,256]{2,1,0:T(8,128)S(1)}, u32[]{:S(2)}, u32[]{:S(2)}) collective-permute-start(f32[2,256,256]{2,1,0:T(8,128)S(1)} %fusion.3), channel_id=1, source_target_pairs={{0,8},{8,16},{16,24},{24,32},{32,40},{40,48},{48,56},{56,64},{64,7... | collective-permute-start | bytes 1572872 | tf_op jit(solution)/shard_map/ppermute | solution.py:12
  282.0 71.3 %collective-permute-start.3 = (f32[2,256,256]{2,1,0:T(8,128)}, f32[2,256,256]{2,1,0:T(8,128)}, u32[]{:S(2)}, u32[]{:S(2)}) collective-permute-start(f32[2,256,256]{2,1,0:T(8,128)} %fusion.1), channel_id=1, source_target_pairs={{0,8},{8,16},{16,24},{24,32},{32,40},{40,48},{48,56},{56,64},{64,7... | collective-permute-start | bytes 1572872 | tf_op jit(solution)/shard_map/ppermute | solution.py:12
  283.6 150.9 %all-reduce.6.cloned.1.call-start = ((), (), s32[]{:S(2)}) async-start(), calls=%async_computation.4 | async-start | bytes 2097152 | tf_op jit(solution)/shard_map/psum | solution.py:79
  351.8 14.1 %collective-permute-start = (f32[2,256,256]{2,1,0:T(8,128)}, f32[2,256,256]{2,1,0:T(8,128)}, u32[]{:S(2)}, u32[]{:S(2)}) collective-permute-start(f32[2,256,256]{2,1,0:T(8,128)} %convolution_subtract_fusion.1), channel_id=1, source_target_pairs={{0,8},{8,16},{16,24},{24,32},{32,40},{40,48},{48,56},{56,64},{64,7... | collective-permute-start | bytes 1572872 | tf_op jit(solution)/shard_map/ppermute | solution.py:12
  355.0 82.5 %copy-start.4 = (f32[2,256,256]{2,1,0:T(8,128)}, f32[2,256,256]{2,1,0:T(8,128)S(1)}, u32[]{:S(2)}) copy-start(f32[2,256,256]{2,1,0:T(8,128)S(1)} %fusion.2) | copy-start | bytes 1572868
  434.5 3.0 copy-start.6
  436.4 2.0 copy-start.5
Sparse Core Ops, SparseCore 0:
  41.5 35.7 all-gather.2
  235.3 38.5 all-gather.4
  283.7 65.0 all-reduce.3
  366.0 68.4 all-reduce.5
where the time goes:
time: 445 us
  waiting for transfers between devices  351 us (79%)
  matrix products  34.3 us (8%)
  local copies, waits for them, and re-layouts  25.7 us (6%)
  starting transfers between devices  18.1 us (4%)
  between operations  14 us (3%)
    ppermute x4, waiting for transfers between devices, shifted(): lax.ppermute(shard, axis, [(i, (i + by) % length) for i in range(length)])  198 us
    psum x1, waiting for transfers between devices, on_device(): cross, back = lax.psum((cross, back), 'row')  67.6 us
    psum x1, waiting for transfers between devices, on_device(): lax.psum(product('kji,kjc->kic', factor1, sel1_panel), 'row')  63.5 us
    dot_general x13, matrix products, product(): return jnp.einsum(form, left, right, precision=HIGH)  34.3 us
    all_gather x1, waiting for transfers between devices, on_device(): lax.all_gather(factor2, 'row', axis=1, tiled=True).reshape(slots, -1, B, B)  21.4 us
    all_to_all x1, starting transfers between devices, on_device(): lax.all_to_all(outgoing, 'own', split_axis=0, concat_axis=0, tiled=True)  11.8 us
    reshape x2, local copies, waits for them, and re-layouts, select_send(): blocks4 = sigma_local.reshape(rows_here, B, cols_here, B)  10.6 us
  transfers between devices with their start and end apart: 9, of which 5 were waited for; matrix products, arithmetic and copies ran while one was open for 9% of the time, Pallas kernels for 0%

commit v1 on v0

--- a/solution.py
+++ b/solution.py
@@ -67,7 +67,9 @@
     gram1 = product("kji,kjc->kic", diag_inv1, diag_inv1)
     sel1_diag = gram1 - lax.psum(product("kji,kjc->kic", factor1, sel1_panel), "row")
     factor2 = keep1[:, :, None] * factor2_child
-    factors2 = lax.all_gather(factor2, "row", axis=1, tiled=True).reshape(slots, -1, B, B)
+    factors2 = jnp.concatenate(
+        lax.all_to_all(jnp.stack([factor2] * lax.axis_size("row")), "row", 0, 0), axis=1
+    ).reshape(slots, -1, B, B)
     anc2 = keep1[:, :, None] * product("kmij,kmjc->kic", blocks1, factors2)
     par_panel = shifted(sel1_panel, "own", 1)
     par_anc = shifted(anc2, "own", 1)

time: 445 us -> 465 us (1.045)
  waiting for transfers between devices: 351 us -> 366 us
    all_to_all x0 -> x1, waiting for transfers between devices: none -> 32.5 us  [on_device(): lax.all_to_all(jnp.stack([factor2] * lax.axis_size('row')), 'row', 0, 0)]
    all_gather x1 -> x0, waiting for transfers between devices: 21.4 us -> none  [on_device(): lax.all_gather(factor2, 'row', axis=1, tiled=True).reshape(slots, -1, B, B)]
where the time goes in v1:
time: 465 us; the launch traced here: 464 us
  waiting for transfers between devices  366 us (79%)
  matrix products  34.3 us (7%)
  local copies, waits for them, and re-layouts  28 us (6%)
  starting transfers between devices  21.1 us (5%)
  between operations  14 us (3%)
    ppermute x4, waiting for transfers between devices, shifted(): lax.ppermute(shard, axis, [(i, (i + by) % length) for i in range(length)])  198 us
    psum x1, waiting for transfers between devices, on_device(): cross, back = lax.psum((cross, back), 'row')  67.6 us
    psum x1, waiting for transfers between devices, on_device(): lax.psum(product('kji,kjc->kic', factor1, sel1_panel), 'row')  67.5 us
    dot_general x13, matrix products, product(): return jnp.einsum(form, left, right, precision=HIGH)  34.3 us
    all_to_all x1, waiting for transfers between devices, on_device(): lax.all_to_all(jnp.stack([factor2] * lax.axis_size('row')), 'row', 0, 0)  32.5 us
    all_to_all x1, starting transfers between devices, on_device(): lax.all_to_all(outgoing, 'own', split_axis=0, concat_axis=0, tiled=True)  11.8 us
    reshape x2, local copies, waits for them, and re-layouts, select_send(): blocks4 = sigma_local.reshape(rows_here, B, cols_here, B)  10.5 us
  transfers between devices with their start and end apart: 9, of which 5 were waited for; matrix products, arithmetic and copies ran while one was open for 9% of the time, Pallas kernels for 0%

profile of v1, /device:TPU:2, one launch (start us, length us, event | category | flops | bytes accessed | tf_op | source)
XLA Modules:
  0.0 464.5 jit_solution(9643945245751888960)
XLA Ops:
  7.2 0.0 copy-start
  7.2 0.8 copy.83
  8.0 0.1 constant_dynamic-slice_fusion
  8.1 0.1 copy.107
  8.2 0.1 copy.85
  8.3 0.1 fusion.15
  8.5 0.7 gather_fusion
  9.1 5.9 %reshape.169 = f32[8,256,2,256]{3,2,1,0:T(2,128)} reshape(f32[2048,512]{1,0:T(8,128)} %param.9) | data formatting | bytes 8388608 | tf_op jit(solution)/shard_map/reshape | solution.py:40
  15.0 4.6 copy.88
  19.7 0.2 fusion.19
  19.9 6.5 %gather_fusion.1 = f32[32,256,256]{2,1,0:T(8,128)} fusion(f32[8,256,2,256]{3,1,2,0:T(8,128)} %copy.88, s32[32]{0:T(128)S(1)} %fusion.19), kind=kCustom, calls=%fused_computation.1 | custom fusion | bytes 16777472 | tf_op jit(solution)/shard_map/gather | solution.py:41
  26.4 0.0 copy-start.8
  26.4 11.8 %all-to-all-start = ((f32[32,256,256]{2,1,0:T(8,128)}), f32[32,256,256]{2,1,0:T(8,128)}, u32[]{:S(2)}, u32[]{:S(2)}) async-start(f32[32,256,256]{2,1,0:T(8,128)} %gather_fusion.1), calls=%async_computation | async-start | bytes 16777216 | tf_op jit(solution)/shard_map/all_to_all | solution.py:61
  38.2 0.0 all-gather.2.cloned.1.call-start
  38.3 0.0 copy-done.9
  38.3 0.0 copy-done.2
  38.3 0.0 copy-done.7
  38.3 1.5 convolution_multiply_fusion.1
  39.8 0.0 all-gather.2.cloned.1.call-update
  39.8 0.0 copy-done.10
  39.8 0.0 copy-done
  39.8 0.0 copy-done.8
  39.8 0.7 convolution_multiply_fusion
  40.5 2.7 collective-permute-start.2
  43.2 190.9 %collective-permute-done.2 = f32[2,256,256]{2,1,0:T(8,128)S(1)} collective-permute-done((f32[2,256,256]{2,1,0:T(8,128)S(1)}, f32[2,256,256]{2,1,0:T(8,128)S(1)}, u32[]{:S(2)}, u32[]{:S(2)}) %collective-permute-start.2) | collective-permute-done | bytes 524320 | tf_op jit(solution)/shard_map/ppermute | solution.py:12
  234.2 0.1 broadcast_multiply_fusion
  234.3 0.0 all-to-all-done
  234.3 2.4 stack.2
  236.7 4.6 all-to-all-start.1
  241.3 0.0 all-reduce.4.cloned.1.call-start
  241.3 0.6 gather_fusion.2
  241.9 0.1 reshape.160
  242.0 6.1 %gather_fusion.3 = f32[16,256,256]{2,1,0:T(8,128)} fusion(f32[32,256,256]{2,1,0:T(8,128)} %all-to-all-done, s32[1024]{0:T(1024)S(1)} %pad_clamp_fusion), kind=kCustom, calls=%fused_computation.3 | custom fusion | bytes 8388672 | tf_op jit(solution)/shard_map/gather | solution.py:48
  248.1 8.1 %fusion.11 = f32[2,256,256]{2,1,0:T(8,128)S(1)} fusion(f32[2,8,256,256]{3,2,1,0:T(8,128)} %bitcast.72, f32[2,8,256,256]{3,2,1,0:T(8,128)} %bitcast.74, f32[2]{0:T(128)S(1)} %fusion.24), kind=kOutput, calls=%fused_computation.17 | convolution fusion | flops 3221356544 | bytes 8912904 | tf_op jit(solution)/shard_map/kmij,kmjc->kic/dot_general | solution.py:16
  256.3 0.0 copy-start.3
  256.3 0.3 collective-permute-start.1
  256.6 0.0 copy-done.1
  256.6 1.9 fusion.26
  258.4 32.5 %all-to-all-done.1 = f32[8,2,256,256]{3,2,1,0:T(8,128)} async-done(((f32[8,2,256,256]{3,2,1,0:T(8,128)}), f32[8,2,256,256]{3,2,1,0:T(8,128)}, u32[]{:S(2)}, u32[]{:S(2)}) %all-to-all-start.1) | async-done | bytes 4194336 | tf_op jit(solution)/shard_map/all_to_all | solution.py:71
  290.9 8.2 %fusion.6 = f32[2,256,256]{2,1,0:T(8,128)} fusion(f32[2,8,256,256]{3,2,1,0:T(8,128)} %bitcast.73, f32[8,2,256,256]{3,2,1,0:T(8,128)} %all-to-all-done.1, f32[2]{0:T(128)S(1)} %convert_bitcast_fusion.1), kind=kOutput, calls=%fused_computation.8 | convolution fusion | flops 3221356544 | bytes 8912904 | tf_op jit(solution)/shard_map/kmij,kmjc->kic/dot_general | solution.py:16
  299.2 0.0 copy-done.3
  299.2 0.0 collective-permute-start.3
  299.2 0.0 all-reduce.4.cloned.1.call-update
  299.2 0.0 all-reduce.6.cloned.1.call-start
  299.2 1.7 fusion.28
  300.9 67.5 %all-reduce.4.cloned.1.call-done = f32[2,256,256]{2,1,0:T(8,128)} async-done(((f32[2,256,256]{2,1,0:T(8,128)}), f32[2,256,256]{2,1,0:T(8,128)}) %all-reduce.4.cloned.1.call-update) | async-done | bytes 524304 | tf_op jit(solution)/shard_map/psum | solution.py:68
  368.4 2.9 convolution_subtract_fusion.1
  371.3 1.6 collective-permute-start
  372.9 0.0 collective-permute-done.3
  372.9 0.0 collective-permute-done.1
  372.9 1.7 fusion.10
  374.6 0.0 copy-start.4
  374.6 1.8 fusion.29
  376.5 1.8 fusion.27
  378.3 7.1 %collective-permute-done = f32[2,256,256]{2,1,0:T(8,128)} collective-permute-done((f32[2,256,256]{2,1,0:T(8,128)}, f32[2,256,256]{2,1,0:T(8,128)}, u32[]{:S(2)}, u32[]{:S(2)}) %collective-permute-start) | collective-permute-done | bytes 524320 | tf_op jit(solution)/shard_map/ppermute | solution.py:12
  385.4 0.0 all-reduce.6.cloned.1.call-update
  385.4 1.1 fusion.30
  386.5 67.6 %all-reduce.6.cloned.1.call-done = (f32[2,256,256]{2,1,0:T(8,128)}, f32[2,256,256]{2,1,0:T(8,128)}) async-done(((f32[2,256,256]{2,1,0:T(8,128)}, f32[2,256,256]{2,1,0:T(8,128)}), (f32[2,256,256]{2,1,0:T(8,128)}, f32[2,256,256]{2,1,0:T(8,128)})) %all-reduce.6.cloned.1.call-update) | async-done | bytes 1048592 | tf_op jit(solution)/shard_map/psum | solution.py:81
  454.1 1.9 fusion.9
  456.0 0.0 copy-start.5
  456.0 1.0 convolution_subtract_fusion
  457.1 0.0 copy-done.4
  457.1 0.9 sub.48
  458.0 0.0 copy-done.5
  (17 shorter events, 0.1 us)
Async XLA Ops:
  7.2 32.7 %copy-start = (f32[2,256,256]{2,1,0:T(8,128)S(1)}, f32[2,256,256]{2,1,0:T(8,128)}, u32[]{:S(2)}) copy-start(f32[2,256,256]{2,1,0:T(8,128)} %param.16) | copy-start | bytes 1572868
  26.4 11.9 %copy-start.9 = (s32[2,1]{0,1:T(1,128)S(1)}, s32[2,1]{0,1:T(1,128)}, u32[]{:S(2)}) copy-start(s32[2,1]{0,1:T(1,128)} %param.13) | copy-start | bytes 28
  26.4 11.9 %copy-start.2 = (f32[2,256,256]{2,1,0:T(8,128)S(1)}, f32[2,256,256]{2,1,0:T(8,128)}, u32[]{:S(2)}) copy-start(f32[2,256,256]{2,1,0:T(8,128)} %param.12) | copy-start | bytes 1572868
  26.4 11.9 %copy-start.7 = (f32[2,256,256]{2,1,0:T(8,128)S(1)}, f32[2,256,256]{2,1,0:T(8,128)}, u32[]{:S(2)}) copy-start(f32[2,256,256]{2,1,0:T(8,128)} %param.11) | copy-start | bytes 1572868
  26.4 13.4 %copy-start.10 = (s32[2,1]{0,1:T(1,128)S(1)}, s32[2,1]{0,1:T(1,128)}, u32[]{:S(2)}) copy-start(s32[2,1]{0,1:T(1,128)} %param.17) | copy-start | bytes 28
  26.4 13.4 %copy-start.8 = (f32[2,256,256]{2,1,0:T(8,128)S(1)}, f32[2,256,256]{2,1,0:T(8,128)}, u32[]{:S(2)}) copy-start(f32[2,256,256]{2,1,0:T(8,128)} %param.15) | copy-start | bytes 1572868
  26.4 207.9 %all-to-all-start = ((f32[32,256,256]{2,1,0:T(8,128)}), f32[32,256,256]{2,1,0:T(8,128)}, u32[]{:S(2)}, u32[]{:S(2)}) async-start(f32[32,256,256]{2,1,0:T(8,128)} %gather_fusion.1), calls=%async_computation | async-start | bytes 16777216 | tf_op jit(solution)/shard_map/all_to_all | solution.py:61
  38.2 209.9 %all-gather.2.cloned.1.call-start = ((), (), s32[]{:S(2)}) async-start(), calls=%async_computation.2 | async-start | bytes 4718592 | tf_op jit(solution)/shard_map/all_gather | solution.py:65
  40.5 193.7 %collective-permute-start.2 = (f32[2,256,256]{2,1,0:T(8,128)S(1)}, f32[2,256,256]{2,1,0:T(8,128)S(1)}, u32[]{:S(2)}, u32[]{:S(2)}) collective-permute-start(f32[2,256,256]{2,1,0:T(8,128)S(1)} %convolution_multiply_fusion), channel_id=1, source_target_pairs={{0,248},{8,0},{16,8},{24,16},{32,24},{40,32},{48,40},{56,48},{64,5... | collective-permute-start | bytes 1572872 | tf_op jit(solution)/shard_map/ppermute | solution.py:12
  236.7 54.3 %all-to-all-start.1 = ((f32[8,2,256,256]{3,2,1,0:T(8,128)}), f32[8,2,256,256]{3,2,1,0:T(8,128)}, u32[]{:S(2)}, u32[]{:S(2)}) async-start(f32[8,2,256,256]{3,2,1,0:T(8,128)} %stack.2), calls=%async_computation.1 | async-start | bytes 8388608 | tf_op jit(solution)/shard_map/all_to_all | solution.py:71
  241.3 127.2 %all-reduce.4.cloned.1.call-start = ((), (), s32[]{:S(2)}) async-start(), calls=%async_computation.3 | async-start | bytes 1048576 | tf_op jit(solution)/shard_map/psum | solution.py:68
  248.1 8.4 %copy-start.1 = (f32[2,256,256]{2,1,0:T(8,128)S(1)}, f32[2,256,256]{2,1,0:T(8,128)}, u32[]{:S(2)}) copy-start(f32[2,256,256]{2,1,0:T(8,128)} %convolution_multiply_fusion.1) | copy-start | bytes 1572868
  256.3 42.9 %copy-start.3 = (f32[2,256,256]{2,1,0:T(8,128)}, f32[2,256,256]{2,1,0:T(8,128)S(1)}, u32[]{:S(2)}) copy-start(f32[2,256,256]{2,1,0:T(8,128)S(1)} %fusion.11) | copy-start | bytes 1572868
  256.3 116.6 %collective-permute-start.1 = (f32[2,256,256]{2,1,0:T(8,128)S(1)}, f32[2,256,256]{2,1,0:T(8,128)S(1)}, u32[]{:S(2)}, u32[]{:S(2)}) collective-permute-start(f32[2,256,256]{2,1,0:T(8,128)S(1)} %fusion.11), channel_id=1, source_target_pairs={{0,8},{8,16},{16,24},{24,32},{32,40},{40,48},{48,56},{56,64},{64,7... | collective-permute-start | bytes 1572872 | tf_op jit(solution)/shard_map/ppermute | solution.py:12
  299.2 73.7 %collective-permute-start.3 = (f32[2,256,256]{2,1,0:T(8,128)}, f32[2,256,256]{2,1,0:T(8,128)}, u32[]{:S(2)}, u32[]{:S(2)}) collective-permute-start(f32[2,256,256]{2,1,0:T(8,128)} %fusion.6), channel_id=1, source_target_pairs={{0,8},{8,16},{16,24},{24,32},{32,40},{40,48},{48,56},{56,64},{64,7... | collective-permute-start | bytes 1572872 | tf_op jit(solution)/shard_map/ppermute | solution.py:12
  299.2 154.9 %all-reduce.6.cloned.1.call-start = ((), (), s32[]{:S(2)}) async-start(), calls=%async_computation.4 | async-start | bytes 2097152 | tf_op jit(solution)/shard_map/psum | solution.py:81
  371.3 14.1 %collective-permute-start = (f32[2,256,256]{2,1,0:T(8,128)}, f32[2,256,256]{2,1,0:T(8,128)}, u32[]{:S(2)}, u32[]{:S(2)}) collective-permute-start(f32[2,256,256]{2,1,0:T(8,128)} %convolution_subtract_fusion.1), channel_id=1, source_target_pairs={{0,8},{8,16},{16,24},{24,32},{32,40},{40,48},{48,56},{56,64},{64,7... | collective-permute-start | bytes 1572872 | tf_op jit(solution)/shard_map/ppermute | solution.py:12
  374.6 82.5 %copy-start.4 = (f32[2,256,256]{2,1,0:T(8,128)}, f32[2,256,256]{2,1,0:T(8,128)S(1)}, u32[]{:S(2)}) copy-start(f32[2,256,256]{2,1,0:T(8,128)S(1)} %fusion.10) | copy-start | bytes 1572868
  454.1 3.0 copy-start.6
  456.0 2.0 copy-start.5
Sparse Core Ops, SparseCore 0:
  41.5 35.7 all-gather.1
  299.3 69.0 all-reduce.3
  385.5 68.4 all-reduce.5
